TPU v7x, 256 devices: a whole 4x4x8 slice. The times are simulated.
256 devices in a mesh: ctx: 8 (over x, core), ch: 32 (over y, z).
Axes of the slice: x: 4, y: 4, z: 8, core: 2. Of those that a mesh axis runs over, the one named last changes fastest.
Arguments:
- tokens_in: bfloat16 [8192, 8192], P(('ctx', 'ch')), may hold values from -6 to 6
- norm_gain: float32 [8192], replicated, may hold values from 0.1 to 1.9
- proj_weight: bfloat16 [3, 8192, 8192], P(None, 'ctx', 'ch'), may hold values from -0.0625 to 0.0625
- conv_weight: float32 [3, 7, 8192], P(None, None, 'ch'), may hold values from -2 to 2
- decay_rate: float32 [16, 8192], P(None, 'ch'), may hold values from 6.1035157e-06 to 0.04
- residue: float32 [16, 8192], P(None, 'ch'), may hold values from -1.5 to 1.5
- skip_gain: float32 [8192], P('ch'), may hold values from -3 to 3
Outputs:
- gated: bfloat16 [8192, 8192], P(('ctx', 'ch'))
All inputs are finite; a program needn't handle non-finite values.
Results may differ from a plain program's by a relative error of at most 0.008.
Values may be sent and summed in bfloat16 or wider, within the bound.
No kernel may reach another device: no remote copies, remote signals or barrier semaphores. Data moves between devices by JAX's collectives and lax.ppermute only.
A program may use at most 128 MiB of HBM per device.

v0:
```python
import jax
import jax.numpy as jnp
from jax import lax
from jax.sharding import PartitionSpec as P

norm_eps = 1e-05


def shifted(shard, axis, by):
    length = lax.axis_size(axis)
    pairs = [(i, i + by) for i in range(length) if 0 <= i + by < length]
    return lax.ppermute(shard, axis, pairs)


def on_device(tokens_in, norm_gain, proj_weight, conv_weight, decay_rate, residue, skip_gain):
    widened = tokens_in.astype(jnp.float32)
    mean_square = jnp.mean(widened * widened, axis=-1, keepdims=True)
    normed = (widened * lax.rsqrt(mean_square + norm_eps) * norm_gain[None, :]).astype(jnp.bfloat16)
    gathered = lax.all_gather(normed, "ch", axis=0, tiled=True)
    row_count = gathered.shape[0]
    chan_count = proj_weight.shape[2]
    summed = jnp.einsum(
        "tf,ifc->itc",
        gathered,
        lax.all_gather(proj_weight, "ctx", axis=1, tiled=True),
        preferred_element_type=jnp.float32,
    )
    projected = summed.astype(jnp.bfloat16)
    tap_count = conv_weight.shape[1]
    reach = tap_count - 1
    rim_rows = shifted(projected[:, row_count - reach :, :], "ctx", 1)
    padded = jnp.concatenate([rim_rows, projected], axis=1).astype(jnp.float32)
    featured = jnp.zeros((3, row_count, chan_count), jnp.float32)
    for shift_idx in range(tap_count):
        featured = (
            featured
            + conv_weight[:, shift_idx, None, :]
            * padded[:, reach - shift_idx : reach - shift_idx + row_count, :]
        )
    queries = featured[0]
    mixed = featured[1] * featured[2]
    highest = lax.Precision.HIGHEST
    in_scale = jnp.sqrt(-jnp.expm1(-2.0 * decay_rate))
    span_rows = min(128, row_count)
    span_count = row_count // span_rows
    positions = jnp.arange(span_rows, dtype=jnp.float32)
    lag_decay = jnp.exp(-decay_rate[:, None, :] * positions[None, :, None])
    impulse = jnp.sum((residue * in_scale)[:, None, :] * lag_decay, axis=0)
    offsets = jnp.arange(span_rows)[:, None] - jnp.arange(span_rows)[None, :]
    lag_table = (offsets[None, :, :] == jnp.arange(span_rows)[:, None, None]).astype(jnp.float32)
    toeplitz = jnp.einsum("lc,lts->cts", impulse, lag_table, precision=highest)
    spans_in = mixed.reshape(span_count, span_rows, chan_count)
    inside = jnp.einsum("cts,jsc->jtc", toeplitz, spans_in, precision=highest)
    end_weight = in_scale[:, None, :] * jnp.exp(
        -decay_rate[:, None, :] * (span_rows - 1.0 - positions)[None, :, None]
    )
    span_ends = jnp.einsum("jsc,msc->jmc", spans_in, end_weight, precision=highest)
    span_decay = jnp.exp(-decay_rate * float(span_rows))

    def advance(carried, span_end):
        return (span_decay * carried + span_end, carried)

    zero_state = jnp.zeros(decay_rate.shape, jnp.float32)
    local_end, starts = lax.scan(advance, zero_state, span_ends)
    whole_decay = jnp.exp(-decay_rate * float(row_count))

    def handoff(unused_turn, incoming):
        return shifted(whole_decay * incoming + local_end, "ctx", 1)

    incoming = lax.fori_loop(0, lax.axis_size("ctx") - 1, handoff, zero_state)
    span_starts = jnp.arange(span_count, dtype=jnp.float32) * float(span_rows)
    starts = (
        starts
        + jnp.exp(-decay_rate[None, :, :] * span_starts[:, None, None]) * incoming[None, :, :]
    )
    out_weight = residue[:, None, :] * jnp.exp(
        -decay_rate[:, None, :] * (positions + 1.0)[None, :, None]
    )
    outside = jnp.einsum("jmc,mtc->jtc", starts, out_weight, precision=highest)
    filtered = (inside + outside).reshape(row_count, chan_count)
    gated = (queries * (filtered + skip_gain[None, :] * mixed)).astype(jnp.bfloat16)
    return lax.all_to_all(gated, "ch", split_axis=0, concat_axis=1, tiled=True)


def solution(mesh):
    in_specs = (
        P(("ctx", "ch"), None),
        P(),
        P(None, "ctx", "ch"),
        P(None, None, "ch"),
        P(None, "ch"),
        P(None, "ch"),
        P("ch"),
    )
    out_specs = P(("ctx", "ch"), None)
    return jax.shard_map(
        on_device, mesh=mesh, in_specs=in_specs, out_specs=out_specs, check_vma=False
    )
```

profile of v0, /device:TPU:34, one launch (start us, length us, event | category | flops | bytes accessed | tf_op | source)
XLA Modules:
  0.0 376.8 jit_solution(1986812862186608656)
XLA Ops:
  8.6 2.0 fusion.40
  12.7 9.6 %fusion.4 = f32[256,128,128]{2,0,1:T(8,128)} fusion(s32[128,128]{1,0:T(8,128)S(1)} %iota_subtract_fusion, f32[128,256]{0,1:T(8,128)S(1)} %multiply_reduce_fusion), kind=kOutput, calls=%fused_computation.8 | convolution fusion | flops 6444548096 | bytes 16973824 | tf_op jit(solution)/shard_map/lc,lts->cts/dot_general | solution.py:51
  22.2 58.8 %all-gather.5.cloned.1.call-done = bf16[3,8192,256]{2,1,0:T(8,128)(2,1)} async-done(((bf16[3,1024,256]{2,1,0:T(8,128)(2,1)}), bf16[3,8192,256]{2,1,0:T(8,128)(2,1)}) %all-gather.5.cloned.1.call-update) | async-done | bytes 12582928 | tf_op jit(solution)/shard_map/all_gather | solution.py:25
  81.0 141.5 %all-gather.3.cloned.1.call-done = bf16[1024,8192]{1,0:T(8,128)(2,1)} async-done(((bf16[32,8192]{1,0:T(8,128)(2,1)}), bf16[1024,8192]{1,0:T(8,128)(2,1)}) %all-gather.3.cloned.1.call-update) | async-done | bytes 16777232 | tf_op jit(solution)/shard_map/all_gather | solution.py:19
  222.6 18.7 %fusion.23 = bf16[3,1024,256]{2,1,0:T(8,128)(2,1)S(1)} fusion(bf16[3,8192,256]{2,1,0:T(8,128)(2,1)} %all-gather.5.cloned.1.call-done, bf16[1024,8192]{1,0:T(8,128)(2,1)} %all-gather.3.cloned.1.call-done), kind=kOutput, calls=%fused_computation.34 | convolution fusion | flops 12885688320 | bytes 30932992 | tf_op jit(solution)/shard_map/tf,ifc->itc/dot_general | solution.py:22
  241.3 2.1 collective-permute-start.1
  244.3 2.0 collective-permute-done.1
  246.6 2.6 fusion.6
  249.8 38.4 %fusion.32 = f32[8,128,256]{1,0,2:T(8,128)} fusion(f32[8,128,256]{1,0,2:T(8,128)S(1)} %copy.29, f32[256,128,128]{2,0,1:T(8,128)} %fusion.4), kind=kOutput, calls=%fused_computation.37 | convolution fusion | flops 402653184 | bytes 18874368 | tf_op jit(solution)/shard_map/cts,jsc->jtc/dot_general | solution.py:53
  288.2 5.2 %fusion.29 = f32[8,16,256]{1,0,2:T(8,128)} fusion(f32[8,128,256]{1,0,2:T(8,128)S(1)} %copy.29, f32[128]{0:T(128)S(1)} %iota_subtract_fusion.1, f32[16,256]{0,1:T(8,128)S(1)} %copy.32, f32[16,256]{0,1:T(8,128)S(1)} %copy.28), kind=kOutput, calls=%fused_computation.36 | convolution fusion | flops 51380224 | bytes 1212928 | tf_op jit(solution)/shard_map/jsc,msc->jmc/dot_general | solution.py:57
  295.0 4.9 %while.24 = (s32[]{:T(128)}, f32[16,256]{1,0:T(8,128)S(1)}, f32[8,16,256]{2,1,0:T(8,128)}, f32[16,256]{1,0:T(8,128)S(1)}, f32[8,16,256]{2,1,0:T(8,128)S(1)}, /*index=5*/s32[]{:T(128)}, s32[]{:T(128)}) while((s32[]{:T(128)}, f32[16,256]{1,0:T(8,128)S(1)}, f32[8,16,256]{2,1,0:T(8,128)}, f32[16,256]{1,0:T(8,128)S(1)}, ...), condition=%wide.region_3.4_spmd.clone, body=%wide.region_2.3_spmd.clone.sunk | while | flops 16387 | bytes 98408 | solution.py:64
  299.9 35.4 %while.23 = (s32[]{:T(128)}, f32[16,256]{1,0:T(8,128)S(1)}, f32[16,256]{1,0:T(8,128)S(1)}, f32[16,256]{1,0:T(8,128)S(1)}, s32[]{:T(128)}) while((s32[]{:T(128)}, f32[16,256]{1,0:T(8,128)S(1)}, f32[16,256]{1,0:T(8,128)S(1)}, f32[16,256]{1,0:T(8,128)S(1)}, s32[]{:T(128)}) %tuple.55), condition=%wide.region_5.6_spmd, body=%wide.region_4.5_spmd.sunk | while | flops 8194 | bytes 131173 | solution.py:70
  299.9 1.9 collective-permute-start
  301.9 3.1 collective-permute-done
  306.9 3.1 collective-permute-done
  312.0 3.1 collective-permute-done
  317.0 3.1 collective-permute-done
  322.1 3.1 collective-permute-done
  325.2 1.9 collective-permute-start
  327.1 3.1 collective-permute-done
  330.3 1.9 collective-permute-start
  332.2 3.1 collective-permute-done
  337.7 5.0 %fusion.35 = f32[8,128,256]{1,0,2:T(8,128)} fusion(f32[8,128,256]{1,0,2:T(8,128)S(1)} %copy-done, f32[8,16,256]{1,0,2:T(8,128)} %copy.35, f32[128]{0:T(128)S(1)} %iota_add_fusion, f32[16,256]{0,1:T(8,128)} %copy.31, f32[16,256]{0,1:T(8,128)S(1)} %copy.28), kind=kOutput, calls=%fused_computation.38 | convolution fusion | flops 51642368 | bytes 2261504 | tf_op jit(solution)/shard_map/jmc,mtc->jtc/dot_general | solution.py:79
  344.6 24.5 %all_to_all.16 = bf16[32,32,256]{2,1,0:T(8,128)(2,1)S(1)} all-to-all(bf16[32,32,256]{2,1,0:T(8,128)(2,1)S(1)} %multiply_convert_fusion), channel_id=1, replica_groups=mesh['ctx'=8,'ch'=32] {'ch'}, dimensions={0} | all-to-all | bytes 1048576 | tf_op jit(solution)/shard_map/all_to_all | solution.py:82
  (71 shorter events, 25.1 us)
Async XLA Ops:
  6.5 4.1 %copy-start.3 = (f32[16,256]{1,0:T(8,128)S(1)}, f32[16,256]{1,0:T(8,128)}, u32[]{:S(2)}) copy-start(f32[16,256]{1,0:T(8,128)} %param.15) | copy-start | bytes 49156
  6.5 4.1 %copy-start.1 = (f32[16,256]{1,0:T(8,128)S(1)}, f32[16,256]{1,0:T(8,128)}, u32[]{:S(2)}) copy-start(f32[16,256]{1,0:T(8,128)} %param.16) | copy-start | bytes 49156
  6.5 6.1 %copy-start.2 = (f32[3,7,256]{2,1,0:T(8,128)S(1)}, f32[3,7,256]{2,1,0:T(8,128)}, u32[]{:S(2)}) copy-start(f32[3,7,256]{2,1,0:T(8,128)} %param.14) | copy-start | bytes 64516
  6.5 74.5 %all-gather.5.cloned.1.call-start = ((), (), s32[]{:S(2)}) async-start(), calls=%async_computation.2 | async-start | bytes 14155776 | tf_op jit(solution)/shard_map/all_gather | solution.py:25
  7.3 215.3 %all-gather.3.cloned.1.call-start = ((), (), s32[]{:S(2)}) async-start(), calls=%async_computation.1 | async-start | bytes 17301504 | tf_op jit(solution)/shard_map/all_gather | solution.py:19
  241.3 5.0 %collective-permute-start.1 = (bf16[3,6,256]{2,1,0:T(8,128)(2,1)S(1)}, bf16[3,6,256]{2,1,0:T(8,128)(2,1)S(1)}, u32[]{:S(2)}, u32[]{:S(2)}) collective-permute-start(bf16[3,6,256]{2,1,0:T(8,128)(2,1)S(1)} %slice.72), channel_id=1, source_target_pairs={{0,32},{32,64},{64,96},{96,128},{128,160},{160,192},{192,224},{1,3... | collective-permute-start | bytes 27656 | tf_op jit(solution)/shard_map/ppermute | solution.py:12
  293.4 44.3 %copy-start = (f32[8,128,256]{1,0,2:T(8,128)S(1)}, f32[8,128,256]{1,0,2:T(8,128)}, u32[]{:S(2)}) copy-start(f32[8,128,256]{1,0,2:T(8,128)} %fusion.32) | copy-start | bytes 3145732
  299.9 5.1 %collective-permute-start = (f32[16,256]{1,0:T(8,128)S(1)}, f32[16,256]{1,0:T(8,128)S(1)}, u32[]{:S(2)}, u32[]{:S(2)}) collective-permute-start(f32[16,256]{1,0:T(8,128)S(1)} %multiply_add_fusion.3), channel_id=1, source_target_pairs={{0,32},{32,64},{64,96},{96,128},{128,160},{160,192},{192,224},{1,3... | collective-permute-start | bytes 49160 | tf_op jit(solution)/shard_map/while/body/eval_jaxpr/ppermute | solution.py:12
  305.0 5.0 %collective-permute-start = (f32[16,256]{1,0:T(8,128)S(1)}, f32[16,256]{1,0:T(8,128)S(1)}, u32[]{:S(2)}, u32[]{:S(2)}) collective-permute-start(f32[16,256]{1,0:T(8,128)S(1)} %multiply_add_fusion.3), channel_id=1, source_target_pairs={{0,32},{32,64},{64,96},{96,128},{128,160},{160,192},{192,224},{1,3... | collective-permute-start | bytes 49160 | tf_op jit(solution)/shard_map/while/body/eval_jaxpr/ppermute | solution.py:12
  310.1 5.0 %collective-permute-start = (f32[16,256]{1,0:T(8,128)S(1)}, f32[16,256]{1,0:T(8,128)S(1)}, u32[]{:S(2)}, u32[]{:S(2)}) collective-permute-start(f32[16,256]{1,0:T(8,128)S(1)} %multiply_add_fusion.3), channel_id=1, source_target_pairs={{0,32},{32,64},{64,96},{96,128},{128,160},{160,192},{192,224},{1,3... | collective-permute-start | bytes 49160 | tf_op jit(solution)/shard_map/while/body/eval_jaxpr/ppermute | solution.py:12
  315.1 5.0 %collective-permute-start = (f32[16,256]{1,0:T(8,128)S(1)}, f32[16,256]{1,0:T(8,128)S(1)}, u32[]{:S(2)}, u32[]{:S(2)}) collective-permute-start(f32[16,256]{1,0:T(8,128)S(1)} %multiply_add_fusion.3), channel_id=1, source_target_pairs={{0,32},{32,64},{64,96},{96,128},{128,160},{160,192},{192,224},{1,3... | collective-permute-start | bytes 49160 | tf_op jit(solution)/shard_map/while/body/eval_jaxpr/ppermute | solution.py:12
  320.2 5.0 %collective-permute-start = (f32[16,256]{1,0:T(8,128)S(1)}, f32[16,256]{1,0:T(8,128)S(1)}, u32[]{:S(2)}, u32[]{:S(2)}) collective-permute-start(f32[16,256]{1,0:T(8,128)S(1)} %multiply_add_fusion.3), channel_id=1, source_target_pairs={{0,32},{32,64},{64,96},{96,128},{128,160},{160,192},{192,224},{1,3... | collective-permute-start | bytes 49160 | tf_op jit(solution)/shard_map/while/body/eval_jaxpr/ppermute | solution.py:12
  325.2 5.0 %collective-permute-start = (f32[16,256]{1,0:T(8,128)S(1)}, f32[16,256]{1,0:T(8,128)S(1)}, u32[]{:S(2)}, u32[]{:S(2)}) collective-permute-start(f32[16,256]{1,0:T(8,128)S(1)} %multiply_add_fusion.3), channel_id=1, source_target_pairs={{0,32},{32,64},{64,96},{96,128},{128,160},{160,192},{192,224},{1,3... | collective-permute-start | bytes 49160 | tf_op jit(solution)/shard_map/while/body/eval_jaxpr/ppermute | solution.py:12
  330.3 5.0 %collective-permute-start = (f32[16,256]{1,0:T(8,128)S(1)}, f32[16,256]{1,0:T(8,128)S(1)}, u32[]{:S(2)}, u32[]{:S(2)}) collective-permute-start(f32[16,256]{1,0:T(8,128)S(1)} %multiply_add_fusion.3), channel_id=1, source_target_pairs={{0,32},{32,64},{64,96},{96,128},{128,160},{160,192},{192,224},{1,3... | collective-permute-start | bytes 49160 | tf_op jit(solution)/shard_map/while/body/eval_jaxpr/ppermute | solution.py:12
  337.7 6.5 %copy-start.4 = (f32[256]{0:T(256)S(1)}, f32[256]{0:T(256)}, u32[]{:S(2)}) copy-start(f32[256]{0:T(256)} %param.17) | copy-start | bytes 3076
Sparse Core Ops, SparseCore 0:
  9.2 71.7 all-gather.4
  83.6 138.9 all-gather.2
where the time goes:
time: 377 us
  waiting for transfers between devices  225 us (60%)
  matrix products  76.7 us (20%)
  blocking collectives  24.5 us (6%)
  starting transfers between devices  15.5 us (4%)
  other arithmetic  14.5 us (4%)
  between operations  13.6 us (4%)
  local copies, waits for them, and re-layouts  6.84 us (2%)
    all_gather x1, waiting for transfers between devices, on_device(): gathered = lax.all_gather(normed, 'ch', axis=0, tiled=True)  142 us
    all_gather x1, waiting for transfers between devices, on_device(): lax.all_gather(proj_weight, 'ctx', axis=1, tiled=True)  58.8 us
    dot_general x1, matrix products, on_device(): inside = jnp.einsum('cts,jsc->jtc', toeplitz, spans_in, precision=highest)  38.4 us
    all_to_all x1, blocking collectives, on_device(): return lax.all_to_all(gated, 'ch', split_axis=0, concat_axis=1, tiled=True)  24.5 us
    ppermute x8, waiting for transfers between devices, shifted(): return lax.ppermute(shard, axis, pairs)  23.9 us
    dot_general x1, matrix products, on_device(): jnp.einsum('tf,ifc->itc', gathered, lax.all_gather(proj_weight, 'ctx', ax...  18.7 us
    ppermute x8, starting transfers between devices, shifted(): return lax.ppermute(shard, axis, pairs)  15.5 us
    dot_general x1, matrix products, on_device(): toeplitz = jnp.einsum('lc,lts->cts', impulse, lag_table, precision=highest)  9.55 us
  transfers between devices with their start and end apart: 10, of which 10 were waited for; matrix products, arithmetic and copies ran while one was open for 4% of the time, Pallas kernels for 0%

commit v1 on v0

--- a/solution.py
+++ b/solution.py
@@ -16,7 +16,12 @@
     widened = tokens_in.astype(jnp.float32)
     mean_square = jnp.mean(widened * widened, axis=-1, keepdims=True)
     normed = (widened * lax.rsqrt(mean_square + norm_eps) * norm_gain[None, :]).astype(jnp.bfloat16)
-    gathered = lax.all_gather(normed, "ch", axis=0, tiled=True)
+    gathered = jnp.concatenate(
+        jax.lax.all_to_all(
+            jnp.stack([normed for _ in range(jax.lax.axis_size("ch"))], axis=0), "ch", 0, 0
+        ),
+        0,
+    )
     row_count = gathered.shape[0]
     chan_count = proj_weight.shape[2]
     summed = jnp.einsum(

time: 377 us -> 593 us (1.57)
  waiting for transfers between devices: 225 us -> 402 us
  blocking collectives: 24.5 us -> 46.9 us
  starting transfers between devices: 15.5 us -> 27.1 us
  local copies, waits for them, and re-layouts: 6.84 us -> 12.8 us
    all_to_all x0 -> x1, waiting for transfers between devices: none -> 317 us  [on_device(): jax.lax.all_to_all(jnp.stack([normed for _ in range(jax.lax.axis_size('ch...]
    all_gather x1 -> x0, waiting for transfers between devices: 142 us -> none  [on_device(): gathered = lax.all_gather(normed, 'ch', axis=0, tiled=True)]
    all_to_all x1, blocking collectives: 24.5 us -> 46.9 us  [on_device(): return lax.all_to_all(gated, 'ch', split_axis=0, concat_axis=1, tiled=True)]
    all_to_all x0 -> x1, starting transfers between devices: none -> 11.5 us  [on_device(): jax.lax.all_to_all(jnp.stack([normed for _ in range(jax.lax.axis_size('ch...]
    another operation x0 -> x1, local copies, waits for them, and re-layouts: none -> 5.99 us  [on_device(): jnp.stack([normed for _ in range(jax.lax.axis_size('ch'))], axis=0)]
  transfers between devices with their start and end apart: 10 -> 10, of which waited for: 10 -> 10; matrix products, arithmetic and copies ran while one was open for 4% -> 2% of each run, Pallas kernels for 0% -> 0%
where the time goes in v1:
time: 593 us
  waiting for transfers between devices  402 us (68%)
  matrix products  76.7 us (13%)
  blocking collectives  46.9 us (8%)
  starting transfers between devices  27.1 us (5%)
  other arithmetic  13.7 us (2%)
  between operations  13.6 us (2%)
  local copies, waits for them, and re-layouts  12.8 us (2%)
    all_to_all x1, waiting for transfers between devices, on_device(): jax.lax.all_to_all(jnp.stack([normed for _ in range(jax.lax.axis_size('ch...  317 us
    all_gather x1, waiting for transfers between devices, on_device(): lax.all_gather(proj_weight, 'ctx', axis=1, tiled=True)  60.6 us
    all_to_all x1, blocking collectives, on_device(): return lax.all_to_all(gated, 'ch', split_axis=0, concat_axis=1, tiled=True)  46.9 us
    dot_general x1, matrix products, on_device(): inside = jnp.einsum('cts,jsc->jtc', toeplitz, spans_in, precision=highest)  38.4 us
    ppermute x8, waiting for transfers between devices, shifted(): return lax.ppermute(shard, axis, pairs)  23.9 us
    dot_general x1, matrix products, on_device(): jnp.einsum('tf,ifc->itc', gathered, lax.all_gather(proj_weight, 'ctx', ax...  18.7 us
    ppermute x8, starting transfers between devices, shifted(): return lax.ppermute(shard, axis, pairs)  15.5 us
  transfers between devices with their start and end apart: 10, of which 10 were waited for; matrix products, arithmetic and copies ran while one was open for 2% of the time, Pallas kernels for 0%

profile of v1, /device:TPU:34, one launch (start us, length us, event | category | flops | bytes accessed | tf_op | source)
XLA Modules:
  0.0 592.7 jit_solution(4145409154433120103)
XLA Ops:
  9.0 6.0 %stack.2 = bf16[32,32,8192]{2,1,0:T(8,128)(2,1)} broadcast(bf16[32,8192]{1,0:T(8,128)(2,1)S(1)} %fusion.33), dimensions={1,2} | broadcast | bytes 17301504 | tf_op jit(solution)/shard_map/stack | solution.py:21
  15.0 11.5 %all-to-all-start = ((bf16[32,32,8192]{2,1,0:T(8,128)(2,1)}), bf16[32,32,8192]{2,1,0:T(8,128)(2,1)}, u32[]{:S(2)}, u32[]{:S(2)}) async-start(bf16[32,32,8192]{2,1,0:T(8,128)(2,1)} %stack.2), calls=%async_computation | async-start | bytes 33554432 | tf_op jit(solution)/shard_map/all_to_all | solution.py:20
  29.4 9.6 %fusion.2 = f32[256,128,128]{2,0,1:T(8,128)} fusion(s32[128,128]{1,0:T(8,128)S(1)} %iota_subtract_fusion, f32[128,256]{0,1:T(8,128)S(1)} %multiply_reduce_fusion), kind=kOutput, calls=%fused_computation.6 | convolution fusion | flops 6444548096 | bytes 16973824 | tf_op jit(solution)/shard_map/lc,lts->cts/dot_general | solution.py:56
  38.9 60.6 %all-gather.2.cloned.1.call-done = bf16[3,8192,256]{2,1,0:T(8,128)(2,1)} async-done(((bf16[3,1024,256]{2,1,0:T(8,128)(2,1)}), bf16[3,8192,256]{2,1,0:T(8,128)(2,1)}) %all-gather.2.cloned.1.call-update) | async-done | bytes 12582928 | tf_op jit(solution)/shard_map/all_gather | solution.py:30
  99.5 316.6 %all-to-all-done = bf16[32,32,8192]{2,1,0:T(8,128)(2,1)} async-done(((bf16[32,32,8192]{2,1,0:T(8,128)(2,1)}), bf16[32,32,8192]{2,1,0:T(8,128)(2,1)}, u32[]{:S(2)}, u32[]{:S(2)}) %all-to-all-start) | async-done | bytes 16777248 | tf_op jit(solution)/shard_map/all_to_all | solution.py:20
  416.1 18.7 %fusion.18 = bf16[3,1024,256]{2,1,0:T(8,128)(2,1)S(1)} fusion(bf16[1024,8192,1]{1,0,2:T(8,128)(2,1)} %bitcast.1, bf16[3,8192,256]{2,1,0:T(8,128)(2,1)} %all-gather.2.cloned.1.call-done), kind=kOutput, calls=%fused_computation.32 | convolution fusion | flops 12885688320 | bytes 30932992 | tf_op jit(solution)/shard_map/tf,ifc->itc/dot_general | solution.py:27
  434.9 2.1 collective-permute-start.1
  437.9 2.0 collective-permute-done.1
  440.2 2.6 fusion.4
  443.4 38.4 %fusion.25 = f32[8,128,256]{1,0,2:T(8,128)} fusion(f32[8,128,256]{1,0,2:T(8,128)S(1)} %copy.29, f32[256,128,128]{2,0,1:T(8,128)} %fusion.2), kind=kOutput, calls=%fused_computation.35 | convolution fusion | flops 402653184 | bytes 18874368 | tf_op jit(solution)/shard_map/cts,jsc->jtc/dot_general | solution.py:58
  481.8 5.2 fusion.22
  488.6 4.9 while.24
  493.5 35.4 %while.23 = (s32[]{:T(128)}, f32[16,256]{1,0:T(8,128)S(1)}, f32[16,256]{1,0:T(8,128)S(1)}, f32[16,256]{1,0:T(8,128)S(1)}, s32[]{:T(128)}) while((s32[]{:T(128)}, f32[16,256]{1,0:T(8,128)S(1)}, f32[16,256]{1,0:T(8,128)S(1)}, f32[16,256]{1,0:T(8,128)S(1)}, s32[]{:T(128)}) %tuple.55), condition=%wide.region_5.6_spmd, body=%wide.region_4.5_spmd.sunk | while | flops 8194 | bytes 131173 | solution.py:75
  493.5 1.9 collective-permute-start
  495.5 3.1 collective-permute-done
  498.6 1.9 collective-permute-start
  500.5 3.1 collective-permute-done
  505.6 3.1 collective-permute-done
  510.6 3.1 collective-permute-done
  515.7 3.1 collective-permute-done
  520.7 3.1 collective-permute-done
  525.8 3.1 collective-permute-done
  531.2 5.0 fusion.28
  538.1 46.9 %all_to_all.21 = bf16[32,32,256]{2,1,0:T(8,128)(2,1)S(1)} all-to-all(bf16[32,32,256]{2,1,0:T(8,128)(2,1)S(1)} %multiply_convert_fusion), channel_id=1, replica_groups=mesh['ctx'=8,'ch'=32] {'ch'}, dimensions={0} | all-to-all | bytes 1048576 | tf_op jit(solution)/shard_map/all_to_all | solution.py:87
  (71 shorter events, 28.2 us)
Async XLA Ops:
  15.0 12.3 %copy-start.1 = (f32[16,256]{1,0:T(8,128)S(1)}, f32[16,256]{1,0:T(8,128)}, u32[]{:S(2)}) copy-start(f32[16,256]{1,0:T(8,128)} %param.16) | copy-start | bytes 49156
  15.0 12.3 %copy-start.3 = (f32[16,256]{1,0:T(8,128)S(1)}, f32[16,256]{1,0:T(8,128)}, u32[]{:S(2)}) copy-start(f32[16,256]{1,0:T(8,128)} %param.15) | copy-start | bytes 49156
  15.0 14.3 %copy-start.2 = (f32[3,7,256]{2,1,0:T(8,128)S(1)}, f32[3,7,256]{2,1,0:T(8,128)}, u32[]{:S(2)}) copy-start(f32[3,7,256]{2,1,0:T(8,128)} %param.14) | copy-start | bytes 64516
  15.0 401.1 %all-to-all-start = ((bf16[32,32,8192]{2,1,0:T(8,128)(2,1)}), bf16[32,32,8192]{2,1,0:T(8,128)(2,1)}, u32[]{:S(2)}, u32[]{:S(2)}) async-start(bf16[32,32,8192]{2,1,0:T(8,128)(2,1)} %stack.2), calls=%async_computation | async-start | bytes 33554432 | tf_op jit(solution)/shard_map/all_to_all | solution.py:20
  26.6 72.9 %all-gather.2.cloned.1.call-start = ((), (), s32[]{:S(2)}) async-start(), calls=%async_computation.2 | async-start | bytes 14155776 | tf_op jit(solution)/shard_map/all_gather | solution.py:30
  434.9 5.0 collective-permute-start.1
  486.9 44.3 %copy-start = (f32[8,128,256]{1,0,2:T(8,128)S(1)}, f32[8,128,256]{1,0,2:T(8,128)}, u32[]{:S(2)}) copy-start(f32[8,128,256]{1,0,2:T(8,128)} %fusion.25) | copy-start | bytes 3145732
  493.5 5.1 collective-permute-start
  498.6 5.0 collective-permute-start
  503.7 5.0 collective-permute-start
  508.7 5.0 collective-permute-start
  513.8 5.0 collective-permute-start
  518.8 5.0 collective-permute-start
  523.9 5.0 collective-permute-start
  531.2 6.5 %copy-start.4 = (f32[256]{0:T(256)S(1)}, f32[256]{0:T(256)}, u32[]{:S(2)}) copy-start(f32[256]{0:T(256)} %param.17) | copy-start | bytes 3076
Sparse Core Ops, SparseCore 0:
  29.2 70.2 all-gather.1
